TPU v7x, 32 devices: a whole 2x2x4 slice. The times are simulated.
32 devices in a mesh: swath: 2 (over y), sub: 4 (over z), beam: 2 (over x), half: 2 (over core).
Axes of the slice: x: 2, y: 2, z: 4, core: 2. Of those that a mesh axis runs over, the one named last changes fastest.
Arguments:
- images: bfloat16 [4, 2, 2048, 1024], P('sub', None, ('swath', 'half'), 'beam'), parts along dimension 2, may hold values from -6 to 6
- offsets: float32 [4], replicated, may hold values from 3840 to 4505
- owners: int32 [2, 4], replicated, may hold values from 0 to 3, each once within a row
Outputs:
- sectors: bfloat16 [8, 1, 2, 512, 2048], P(('sub', 'beam'), None, None, None, ('swath', 'half')), parts along dimension 4
There are 2 independent parts, one for each index of `swath`. A program takes and returns all parts, laid end to end along the dimension named above; an argument that names none is the same for every part. Nothing has to cross between parts.
Inputs may be any that keep to these rules, and one draw needn't show every extreme that they name: Each row of owners names every one of the 4 sectors of its beam shard exactly once.
All inputs are finite; a program needn't handle non-finite values.
Results may differ from a plain program's by a relative error of at most 0.0052.
Values may be sent and summed in bfloat16 or wider, within the bound.
No kernel may reach another device: no remote copies, remote signals or barrier semaphores. Data moves between devices by JAX's collectives and lax.ppermute only.
A program may use at most 64 MiB of HBM per device.

v0:
```python
import math
import jax
import jax.numpy as jnp
from jax import lax
from jax.sharding import PartitionSpec as P

B = 1024
NR = 1024


def swapped(value, axis, distance):
    return lax.ppermute(value, axis, [(i, i ^ 1 << distance) for i in range(lax.axis_size(axis))])


def odd_kernel(beam_total, columns):
    source_ix = lax.broadcasted_iota(jnp.int32, (beam_total, columns), 0)
    target_ix = lax.broadcasted_iota(jnp.int32, (beam_total, columns), 1)
    spacing = target_ix - source_ix
    parity = jnp.where(spacing % 2 == 0, 1.0, -1.0).astype(jnp.float32)
    angles = (2.0 * spacing.astype(jnp.float32) + 1.0) * (math.pi / (2.0 * beam_total))
    return (parity * jnp.cos(angles) / (beam_total * jnp.sin(angles))).astype(jnp.bfloat16)


def steer_phase(upsampled, shifts, rows_at, beams_at, beams_out):
    ratios = NR / (NR + rows_at.astype(jnp.float32))
    tilts = (2.0 * beams_at.astype(jnp.float32) + 1.0) / beams_out - 1.0
    phases = ratios[:, None] * tilts[None, :] * shifts[..., None, None]
    cosine = jnp.cos(phases)
    sines = jnp.sin(phases)
    real_part = upsampled[..., 0, :, :]
    imag_part = upsampled[..., 1, :, :]
    return jnp.stack(
        [real_part * cosine - imag_part * sines, real_part * sines + imag_part * cosine], -3
    )


def rotate_sum(children, odd_beams, shifts, rows_at, beams_out):
    count = children.shape[-1]
    even_at = 2 * jnp.arange(count, dtype=jnp.int32)
    even_sum = jnp.sum(
        steer_phase(children.astype(jnp.float32), shifts, rows_at, even_at, beams_out), axis=0
    )
    odd_sum = jnp.sum(steer_phase(odd_beams, shifts, rows_at, even_at + 1, beams_out), axis=0)
    joined = jnp.stack([even_sum, odd_sum], -1)
    return joined.reshape(even_sum.shape[:-1] + (2 * count,)).astype(jnp.bfloat16)


def odd_local(children, kernel):
    product = jnp.dot(
        children.reshape(-1, children.shape[-1]), kernel, preferred_element_type=jnp.float32
    )
    return product.reshape(children.shape[:-1] + (kernel.shape[1],))


def swap_first(pieces):
    return swapped(pieces, "sub", 0)


def swap_second(pieces):
    return swapped(pieces, "sub", 1)


def keep_and_trade(field, which_bit, swapper):
    length = field.shape[2] // 2
    kept = lax.dynamic_slice_in_dim(field, which_bit * length, length, 2)
    given = lax.dynamic_slice_in_dim(field, (1 - which_bit) * length, length, 2)
    return (jnp.stack([kept, swapper(given)]), length)


def shift_block(offsets, index, per_device):
    return lax.dynamic_slice_in_dim(offsets, index * per_device, per_device, 0)


def body(images, offsets, owners):
    sub_count = lax.axis_size("sub")
    beam_count = lax.axis_size("beam")
    sub_place = lax.axis_index("sub")
    beam_lane = lax.axis_index("beam")
    half_side = lax.axis_index("half")
    low_bit = sub_place % 2
    high_bit = sub_place // 2 % 2
    per_device = images.shape[0]
    half_rows = images.shape[2]
    own_shift = shift_block(offsets, sub_place, per_device)
    mate_shift = shift_block(offsets, jnp.bitwise_xor(sub_place, 1), per_device)
    shifts_one = jnp.stack([own_shift, mate_shift])
    pair_base = sub_place - low_bit
    mate_base = jnp.bitwise_xor(sub_place, 2) - low_bit
    center_own = (
        shift_block(offsets, pair_base, per_device)
        + shift_block(offsets, pair_base + 1, per_device)
    ) * 0.5
    center_mate = (
        shift_block(offsets, mate_base, per_device)
        + shift_block(offsets, mate_base + 1, per_device)
    ) * 0.5
    shifts_two = jnp.stack([center_own, center_mate])
    all_beams = lax.all_to_all(images, "beam", split_axis=2, concat_axis=3, tiled=True)
    block_rows = all_beams.shape[2]
    start_row = half_side * half_rows + beam_lane * block_rows
    children, length = keep_and_trade(all_beams, low_bit, swap_first)
    rows_at = start_row + low_bit * length + jnp.arange(length, dtype=jnp.int32)
    odd_beams = odd_local(children, odd_kernel(B, B))
    first_merge = rotate_sum(children, odd_beams, shifts_one, rows_at, 2 * B)
    children, quarter = keep_and_trade(first_merge, high_bit, swap_second)
    rows_at = (
        start_row + low_bit * length + high_bit * quarter + jnp.arange(quarter, dtype=jnp.int32)
    )
    odd_beams = odd_local(children, odd_kernel(2 * B, 2 * B))
    merged = rotate_sum(children, odd_beams, shifts_two, rows_at, 4 * B)
    sector_tiles = merged.reshape(per_device, 2, quarter, beam_count, sub_count, -1)
    beam_ids = jnp.arange(beam_count, dtype=jnp.int32)[:, None]
    picked = sector_tiles[:, :, :, beam_ids, owners, :]
    outgoing = picked.transpose(4, 3, 0, 1, 5, 2)
    received = lax.all_to_all(
        lax.all_to_all(outgoing, "sub", split_axis=0, concat_axis=0, tiled=True),
        "beam",
        split_axis=1,
        concat_axis=1,
        tiled=True,
    )
    sector_width = received.shape[4]
    received = received.reshape(
        sub_count // 4, 2, 2, beam_count, per_device, 2, sector_width, quarter
    )
    received = received.transpose(0, 4, 5, 6, 3, 2, 1, 7)
    return received.reshape(1, sub_count // 4 * per_device, 2, sector_width, half_rows)


def solution(mesh):
    placed = (P("sub", None, ("swath", "half"), "beam"), P(), P())
    return jax.shard_map(
        body,
        mesh=mesh,
        in_specs=placed,
        out_specs=P(("sub", "beam"), None, None, None, ("swath", "half")),
        check_vma=False,
    )
```

profile of v0, /device:TPU:0, one launch (start us, length us, event | category | flops | bytes accessed | tf_op | source)
XLA Modules:
  0.0 222.6 jit_solution(12710477142224495665)
XLA Ops:
  0.0 3.3 %copy.32 = bf16[1,2,512,512]{3,1,0,2:T(2,128)(2,1)} copy(bf16[1,2,512,512]{3,2,1,0:T(8,128)(2,1)} %param.3) | data formatting | bytes 2097152 | tf_op args[0]
  3.3 4.2 %all-to-all-start = ((bf16[1,2,512,512]{3,1,0,2:T(2,128)(2,1)}), bf16[1,2,512,512]{3,1,0,2:T(2,128)(2,1)S(1)}, u32[]{:S(2)}, u32[]{:S(2)}) async-start(bf16[1,2,512,512]{3,1,0,2:T(2,128)(2,1)} %copy.32), calls=%async_computation | async-start | bytes 2097152 | tf_op jit(solution)/shard_map/all_to_all | solution.py:98
  7.5 0.7 fusion.82
  8.2 13.7 %all-to-all-done = bf16[1,2,512,512]{3,1,0,2:T(2,128)(2,1)S(1)} async-done(((bf16[1,2,512,512]{3,1,0,2:T(2,128)(2,1)}), bf16[1,2,512,512]{3,1,0,2:T(2,128)(2,1)S(1)}, u32[]{:S(2)}, u32[]{:S(2)}) %all-to-all-start) | async-done | bytes 1048608 | tf_op jit(solution)/shard_map/all_to_all | solution.py:98
  22.0 1.1 copy.50
  23.1 1.2 all_to_all.22
  24.4 1.9 collective-permute-start
  26.3 1.3 maximum_bitcast_fusion
  30.1 0.1 broadcast_multiply_fusion.3
  30.2 7.3 %collective-permute-done = bf16[1,2,128,1024]{3,2,1,0:T(8,128)(2,1)S(1)} collective-permute-done((bf16[1,2,128,1024]{3,2,1,0:T(8,128)(2,1)S(1)}, bf16[1,2,128,1024]{3,2,1,0:T(8,128)(2,1)S(1)}, u32[]{:S(2)}, u32[]{:S(2)}) %collective-permute-start) | collective-permute-done | bytes 524320 | tf_op jit(solution)/shard_map/ppermute | solution.py:12
  37.5 17.8 %fusion.29 = f32[2,1,2,128,1024]{4,3,2,0,1:T(8,128)S(1)} fusion(bf16[1,1,2,128,1024]{4,3,2,0,1:T(8,128)(2,1)S(1)} %bitcast.99, bf16[1,1,2,128,1024]{4,3,2,0,1:T(8,128)(2,1)S(1)} %get-tuple-element.15), kind=kOutput, calls=%fused_computation.40 | convolution fusion | flops 1097334784 | bytes 3145728 | tf_op jit(solution)/shard_map/dot_general | solution.py:49
  55.4 0.1 fusion.59
  55.5 8.0 %fusion.54 = (f32[2,1,1,128,1024]{4,3,2,0,1:T(8,128)S(1)}, f32[2,1,1,128,1024]{4,3,2,0,1:T(8,128)S(1)}, f32[2,1,1,128,1024]{4,3,2,0,1:T(8,128)S(1)}, f32[2,1,1,128,1024]{4,3,2,0,1:T(8,128)S(1)}) fusion(f32[2,1,2,128,1024]{4,3,2,0,1:T(8,128)S(1)} %fusion.59, f32[2]{0:T(128)S(1)} %maximum_bitcast_fusion, f32[128,1024]{1,0:T(8,128)S(1)} %get-tuple-element.29, ...), kind=kLoop, calls=%fused_computation.71 | loop fusion | flops 3670016 | bytes 9437192 | tf_op jit(solution)/shard_map/sub | solution.py:33
  63.5 0.1 maximum_reduce_fusion
  63.7 0.1 maximum_reduce_fusion.1
  63.9 0.8 copy.34
  64.7 0.6 constant_dynamic-slice_fusion.1
  65.4 1.1 copy.46
  66.5 2.6 %collective-permute-start.1 = (bf16[1,2,64,2048]{3,2,1,0:T(8,128)(2,1)}, bf16[1,2,64,2048]{3,2,1,0:T(8,128)(2,1)S(1)}, u32[]{:S(2)}, u32[]{:S(2)}) collective-permute-start(bf16[1,2,64,2048]{3,2,1,0:T(8,128)(2,1)} %copy.46), channel_id=1, source_target_pairs={{0,8},{4,12},{8,0},{12,4},{1,9},{5,13},{9,1},{13,5},{2,10},{6,14},... | collective-permute-start | bytes 1572872 | tf_op jit(solution)/shard_map/ppermute | solution.py:12
  69.2 0.2 broadcast_multiply_fusion.1
  69.4 0.3 copy.35
  69.7 21.4 %collective-permute-done.1 = bf16[1,2,64,2048]{3,2,1,0:T(8,128)(2,1)S(1)} collective-permute-done((bf16[1,2,64,2048]{3,2,1,0:T(8,128)(2,1)}, bf16[1,2,64,2048]{3,2,1,0:T(8,128)(2,1)S(1)}, u32[]{:S(2)}, u32[]{:S(2)}) %collective-permute-start.1) | collective-permute-done | bytes 524320 | tf_op jit(solution)/shard_map/ppermute | solution.py:12
  91.2 0.1 fusion.58
  91.3 72.2 %fusion.15 = f32[2,1,2,64,2048]{4,3,2,0,1:T(8,128)S(1)} fusion(bf16[2,2,64,2048]{3,2,1,0:T(8,128)(2,1)S(1)} %fusion.89), kind=kOutput, calls=%fused_computation.25 | convolution fusion | flops 2239758336 | bytes 3145728 | tf_op jit(solution)/shard_map/dot_general | solution.py:49
  163.5 8.0 %fusion.50 = (f32[2,1,1,64,2048]{4,3,2,0,1:T(8,128)S(1)}, f32[2,1,1,64,2048]{4,3,2,0,1:T(8,128)S(1)}, f32[2,1,1,64,2048]{4,3,2,0,1:T(8,128)S(1)}, f32[2,1,1,64,2048]{4,3,2,0,1:T(8,128)S(1)}) fusion(f32[2,1,2,64,2048]{4,3,2,0,1:T(8,128)S(1)} %fusion.58, f32[2]{0:T(128)S(1)} %maximum_bitcast_fusion.1, f32[64,2048]{1,0:T(8,128)S(1)} %get-tuple-element.19, ...), kind=kLoop, calls=%fused_computation.67 | loop fusion | flops 3670016 | bytes 9437192 | tf_op jit(solution)/shard_map/sub | solution.py:33
  171.5 0.1 maximum_reduce_fusion.2
  171.9 1.5 copy.37
  173.4 0.8 copy.38
  174.2 0.6 gather_fusion
  175.0 30.2 %all_to_all.28 = bf16[4,2,1,2,512,64]{4,5,3,2,1,0:T(8,128)(2,1)S(1)} all-to-all(bf16[4,2,1,2,512,64]{4,5,3,2,1,0:T(8,128)(2,1)S(1)} %bitcast.90), channel_id=1, replica_groups=mesh['swath'=2,'sub'=4,'beam'=2,'half'=2] {'sub'}, dimensions={0} | all-to-all | bytes 2097152 | tf_op jit(solution)/shard_map/all_to_all | solution.py:116
  205.2 15.6 %all_to_all.29 = bf16[4,2,1,2,512,64]{4,5,3,2,0,1:T(8,128)(2,1)S(1)} all-to-all(bf16[4,2,1,2,512,64]{4,5,3,2,0,1:T(8,128)(2,1)S(1)} %copy.40), channel_id=1, replica_groups=mesh['swath'=2,'sub'=4,'beam'=2,'half'=2] {'beam'}, dimensions={1} | all-to-all | bytes 2097152 | tf_op jit(solution)/shard_map/all_to_all | solution.py:115
  221.0 1.3 copy.43
  (20 shorter events, 1.1 us)
Async XLA Ops:
  0.0 7.5 %copy-start = (f32[4]{0:T(128)S(1)}, f32[4]{0:T(128)}, u32[]{:S(2)}) copy-start(f32[4]{0:T(128)} %param.4) | copy-start | bytes 52
  3.3 18.7 %all-to-all-start = ((bf16[1,2,512,512]{3,1,0,2:T(2,128)(2,1)}), bf16[1,2,512,512]{3,1,0,2:T(2,128)(2,1)S(1)}, u32[]{:S(2)}, u32[]{:S(2)}) async-start(bf16[1,2,512,512]{3,1,0,2:T(2,128)(2,1)} %copy.32), calls=%async_computation | async-start | bytes 2097152 | tf_op jit(solution)/shard_map/all_to_all | solution.py:98
  23.0 7.0 %copy-start.1 = (s32[2,4]{1,0:T(2,128)S(1)}, s32[2,4]{1,0:T(2,128)}, u32[]{:S(2)}) copy-start(s32[2,4]{1,0:T(2,128)} %param.5) | copy-start | bytes 100
  24.4 13.2 %collective-permute-start = (bf16[1,2,128,1024]{3,2,1,0:T(8,128)(2,1)S(1)}, bf16[1,2,128,1024]{3,2,1,0:T(8,128)(2,1)S(1)}, u32[]{:S(2)}, u32[]{:S(2)}) collective-permute-start(bf16[1,2,128,1024]{3,2,1,0:T(8,128)(2,1)S(1)} %get-tuple-element.16), channel_id=1, source_target_pairs={{0,4},{4,0},{8,12},{12,8},{1,5},{5,1},{9,13},{13,9},{2,6},{6,2},{1... | collective-permute-start | bytes 1572872 | tf_op jit(solution)/shard_map/ppermute | solution.py:12
  66.5 24.6 %collective-permute-start.1 = (bf16[1,2,64,2048]{3,2,1,0:T(8,128)(2,1)}, bf16[1,2,64,2048]{3,2,1,0:T(8,128)(2,1)S(1)}, u32[]{:S(2)}, u32[]{:S(2)}) collective-permute-start(bf16[1,2,64,2048]{3,2,1,0:T(8,128)(2,1)} %copy.46), channel_id=1, source_target_pairs={{0,8},{4,12},{8,0},{12,4},{1,9},{5,13},{9,1},{13,5},{2,10},{6,14},... | collective-permute-start | bytes 1572872 | tf_op jit(solution)/shard_map/ppermute | solution.py:12
where the time goes:
time: 226 us; the launch traced here: 223 us
  matrix products  90 us (40%)
  blocking collectives  45.8 us (20%)
  waiting for transfers between devices  42.4 us (19%)
  other arithmetic  18.8 us (8%)
  local copies, waits for them, and re-layouts  14 us (6%)
  starting transfers between devices  8.68 us (4%)
  between operations  2.96 us (1%)
    dot_general x2, matrix products, odd_local(): jnp.dot(children.reshape(-1, children.shape[-1]), kernel, preferred_eleme...  90 us
    all_to_all x1, blocking collectives, body(): lax.all_to_all(outgoing, 'sub', split_axis=0, concat_axis=0, tiled=True)  30.2 us
    ppermute x2, waiting for transfers between devices, swapped(): lax.ppermute(value, axis, [(i, i ^ 1 << distance) for i in range(lax.axis...  28.7 us
    sub x2, other arithmetic, steer_phase(): real_part * cosine - imag_part * sines  16 us
    all_to_all x1, blocking collectives, body(): lax.all_to_all(lax.all_to_all(outgoing, 'sub', split_axis=0, concat_axis=...  15.6 us
    all_to_all x1, waiting for transfers between devices, body(): lax.all_to_all(images, 'beam', split_axis=2, concat_axis=3, tiled=True)  13.7 us
  transfers between devices with their start and end apart: 3, of which 3 were waited for; matrix products, arithmetic and copies ran while one was open for 1% of the time, Pallas kernels for 0%

commit v1 on v0

--- a/solution.py
+++ b/solution.py
@@ -3,6 +3,7 @@
 import jax.numpy as jnp
 from jax import lax
 from jax.sharding import PartitionSpec as P
+from jax.lax import all_to_all, psum
 
 B = 1024
 NR = 1024
@@ -112,13 +113,12 @@
     beam_ids = jnp.arange(beam_count, dtype=jnp.int32)[:, None]
     picked = sector_tiles[:, :, :, beam_ids, owners, :]
     outgoing = picked.transpose(4, 3, 0, 1, 5, 2)
-    received = lax.all_to_all(
-        lax.all_to_all(outgoing, "sub", split_axis=0, concat_axis=0, tiled=True),
-        "beam",
-        split_axis=1,
-        concat_axis=1,
-        tiled=True,
-    )
+    payload = lax.all_to_all(outgoing, "sub", split_axis=0, concat_axis=0, tiled=True)
+    odd = psum(1, "beam")
+    carry_in = jnp.split(payload, odd, axis=1)
+    long_array = jnp.stack(carry_in, axis=0)
+    z1 = all_to_all(long_array, "beam", 0, 0)
+    received = jnp.concatenate(z1, axis=1)
     sector_width = received.shape[4]
     received = received.reshape(
         sub_count // 4, 2, 2, beam_count, per_device, 2, sector_width, quarter

time: 226 us -> 226 us (level)
  no operation moved by 1% of the time
where the time goes in v1:
time: 226 us; the launch traced here: 223 us
  matrix products  90 us (40%)
  blocking collectives  45.8 us (20%)
  waiting for transfers between devices  42.4 us (19%)
  other arithmetic  19 us (8%)
  local copies, waits for them, and re-layouts  14 us (6%)
  starting transfers between devices  8.68 us (4%)
  between operations  2.92 us (1%)
    dot_general x2, matrix products, odd_local(): jnp.dot(children.reshape(-1, children.shape[-1]), kernel, preferred_eleme...  90 us
    all_to_all x1, blocking collectives, body(): lax.all_to_all(outgoing, 'sub', split_axis=0, concat_axis=0, tiled=True)  30.2 us
    ppermute x2, waiting for transfers between devices, swapped(): lax.ppermute(value, axis, [(i, i ^ 1 << distance) for i in range(lax.axis...  28.6 us
    sub x2, other arithmetic, steer_phase(): real_part * cosine - imag_part * sines  16 us
    all_to_all x1, blocking collectives, body(): z1 = all_to_all(long_array, 'beam', 0, 0)  15.6 us
    all_to_all x1, waiting for transfers between devices, body(): lax.all_to_all(images, 'beam', split_axis=2, concat_axis=3, tiled=True)  13.7 us
  transfers between devices with their start and end apart: 3, of which 3 were waited for; matrix products, arithmetic and copies ran while one was open for 1% of the time, Pallas kernels for 0%

profile of v1, /device:TPU:0, one launch (start us, length us, event | category | flops | bytes accessed | tf_op | source)
XLA Modules:
  0.0 222.7 jit_solution(11036074471717078610)
XLA Ops:
  0.0 3.3 %copy.23 = bf16[1,2,512,512]{3,1,0,2:T(2,128)(2,1)} copy(bf16[1,2,512,512]{3,2,1,0:T(8,128)(2,1)} %param.3) | data formatting | bytes 2097152 | tf_op args[0]
  3.3 4.2 %all-to-all-start = ((bf16[1,2,512,512]{3,1,0,2:T(2,128)(2,1)}), bf16[1,2,512,512]{3,1,0,2:T(2,128)(2,1)S(1)}, u32[]{:S(2)}, u32[]{:S(2)}) async-start(bf16[1,2,512,512]{3,1,0,2:T(2,128)(2,1)} %copy.23), calls=%async_computation | async-start | bytes 2097152 | tf_op jit(solution)/shard_map/all_to_all | solution.py:99
  7.5 0.7 fusion.82
  8.3 13.7 %all-to-all-done = bf16[1,2,512,512]{3,1,0,2:T(2,128)(2,1)S(1)} async-done(((bf16[1,2,512,512]{3,1,0,2:T(2,128)(2,1)}), bf16[1,2,512,512]{3,1,0,2:T(2,128)(2,1)S(1)}, u32[]{:S(2)}, u32[]{:S(2)}) %all-to-all-start) | async-done | bytes 1048608 | tf_op jit(solution)/shard_map/all_to_all | solution.py:99
  22.0 1.1 copy.43
  23.1 1.2 all_to_all.22
  24.4 1.9 collective-permute-start
  26.3 1.4 maximum_bitcast_fusion.1
  30.1 0.1 broadcast_multiply_fusion.3
  30.3 7.3 %collective-permute-done = bf16[1,2,128,1024]{3,2,1,0:T(8,128)(2,1)S(1)} collective-permute-done((bf16[1,2,128,1024]{3,2,1,0:T(8,128)(2,1)S(1)}, bf16[1,2,128,1024]{3,2,1,0:T(8,128)(2,1)S(1)}, u32[]{:S(2)}, u32[]{:S(2)}) %collective-permute-start) | collective-permute-done | bytes 524320 | tf_op jit(solution)/shard_map/ppermute | solution.py:13
  37.5 17.8 %fusion.29 = f32[2,1,2,128,1024]{4,3,2,0,1:T(8,128)S(1)} fusion(bf16[1,1,2,128,1024]{4,3,2,0,1:T(8,128)(2,1)S(1)} %bitcast.109, bf16[1,1,2,128,1024]{4,3,2,0,1:T(8,128)(2,1)S(1)} %get-tuple-element.17), kind=kOutput, calls=%fused_computation.40 | convolution fusion | flops 1097334784 | bytes 3145728 | tf_op jit(solution)/shard_map/dot_general | solution.py:50
  55.4 0.1 fusion.59
  55.5 8.0 %fusion.54 = (f32[2,1,1,128,1024]{4,3,2,0,1:T(8,128)S(1)}, f32[2,1,1,128,1024]{4,3,2,0,1:T(8,128)S(1)}, f32[2,1,1,128,1024]{4,3,2,0,1:T(8,128)S(1)}, f32[2,1,1,128,1024]{4,3,2,0,1:T(8,128)S(1)}) fusion(f32[2,1,2,128,1024]{4,3,2,0,1:T(8,128)S(1)} %fusion.59, f32[2]{0:T(128)S(1)} %maximum_bitcast_fusion.1, f32[128,1024]{1,0:T(8,128)S(1)} %get-tuple-element.31, ...), kind=kLoop, calls=%fused_computation.71 | loop fusion | flops 3670016 | bytes 9437192 | tf_op jit(solution)/shard_map/sub | solution.py:34
  63.5 0.1 maximum_reduce_fusion
  63.7 0.1 maximum_reduce_fusion.1
  63.9 0.8 copy.25
  64.7 0.6 constant_dynamic-slice_fusion.1
  65.4 1.1 copy.38
  66.5 2.6 %collective-permute-start.1 = (bf16[1,2,64,2048]{3,2,1,0:T(8,128)(2,1)}, bf16[1,2,64,2048]{3,2,1,0:T(8,128)(2,1)S(1)}, u32[]{:S(2)}, u32[]{:S(2)}) collective-permute-start(bf16[1,2,64,2048]{3,2,1,0:T(8,128)(2,1)} %copy.38), channel_id=1, source_target_pairs={{0,8},{4,12},{8,0},{12,4},{1,9},{5,13},{9,1},{13,5},{2,10},{6,14},... | collective-permute-start | bytes 1572872 | tf_op jit(solution)/shard_map/ppermute | solution.py:13
  69.2 0.2 broadcast_multiply_fusion.1
  69.4 0.3 copy.26
  69.7 21.4 %collective-permute-done.1 = bf16[1,2,64,2048]{3,2,1,0:T(8,128)(2,1)S(1)} collective-permute-done((bf16[1,2,64,2048]{3,2,1,0:T(8,128)(2,1)}, bf16[1,2,64,2048]{3,2,1,0:T(8,128)(2,1)S(1)}, u32[]{:S(2)}, u32[]{:S(2)}) %collective-permute-start.1) | collective-permute-done | bytes 524320 | tf_op jit(solution)/shard_map/ppermute | solution.py:13
  91.2 0.1 fusion.58
  91.3 72.2 %fusion.15 = f32[2,1,2,64,2048]{4,3,2,0,1:T(8,128)S(1)} fusion(bf16[2,2,64,2048]{3,2,1,0:T(8,128)(2,1)S(1)} %fusion.89), kind=kOutput, calls=%fused_computation.25 | convolution fusion | flops 2239758336 | bytes 3145728 | tf_op jit(solution)/shard_map/dot_general | solution.py:50
  163.5 8.0 %fusion.50 = (f32[2,1,1,64,2048]{4,3,2,0,1:T(8,128)S(1)}, f32[2,1,1,64,2048]{4,3,2,0,1:T(8,128)S(1)}, f32[2,1,1,64,2048]{4,3,2,0,1:T(8,128)S(1)}, f32[2,1,1,64,2048]{4,3,2,0,1:T(8,128)S(1)}) fusion(f32[2,1,2,64,2048]{4,3,2,0,1:T(8,128)S(1)} %fusion.58, f32[2]{0:T(128)S(1)} %maximum_bitcast_fusion.2, f32[64,2048]{1,0:T(8,128)S(1)} %get-tuple-element.21, ...), kind=kLoop, calls=%fused_computation.67 | loop fusion | flops 3670016 | bytes 9437192 | tf_op jit(solution)/shard_map/sub | solution.py:34
  171.5 0.1 maximum_reduce_fusion.2
  171.9 1.5 copy.28
  173.4 0.8 copy.29
  174.2 0.6 gather_fusion
  175.0 30.2 %all_to_all.28 = bf16[4,2,1,2,512,64]{4,5,3,2,1,0:T(8,128)(2,1)S(1)} all-to-all(bf16[4,2,1,2,512,64]{4,5,3,2,1,0:T(8,128)(2,1)S(1)} %bitcast.100), channel_id=1, replica_groups=mesh['swath'=2,'sub'=4,'beam'=2,'half'=2] {'sub'}, dimensions={0} | all-to-all | bytes 2097152 | tf_op jit(solution)/shard_map/all_to_all | solution.py:116
  205.3 15.6 %all_to_all.29 = bf16[2,4,1,1,2,512,64]{5,6,4,3,2,1,0:T(8,128)(2,1)S(1)} all-to-all(bf16[2,4,1,1,2,512,64]{5,6,4,3,2,1,0:T(8,128)(2,1)S(1)} %maximum_bitcast_fusion), channel_id=1, replica_groups=mesh['swath'=2,'sub'=4,'beam'=2,'half'=2] {'beam'}, dimensions={0} | all-to-all | bytes 2097152 | tf_op jit(solution)/shard_map/all_to_all | solution.py:120
  221.1 1.3 copy.35
  (21 shorter events, 1.2 us)
Async XLA Ops:
  0.0 7.5 %copy-start = (f32[4]{0:T(128)S(1)}, f32[4]{0:T(128)}, u32[]{:S(2)}) copy-start(f32[4]{0:T(128)} %param.4) | copy-start | bytes 52
  3.3 18.7 %all-to-all-start = ((bf16[1,2,512,512]{3,1,0,2:T(2,128)(2,1)}), bf16[1,2,512,512]{3,1,0,2:T(2,128)(2,1)S(1)}, u32[]{:S(2)}, u32[]{:S(2)}) async-start(bf16[1,2,512,512]{3,1,0,2:T(2,128)(2,1)} %copy.23), calls=%async_computation | async-start | bytes 2097152 | tf_op jit(solution)/shard_map/all_to_all | solution.py:99
  23.0 7.0 %copy-start.1 = (s32[2,4]{1,0:T(2,128)S(1)}, s32[2,4]{1,0:T(2,128)}, u32[]{:S(2)}) copy-start(s32[2,4]{1,0:T(2,128)} %param.5) | copy-start | bytes 100
  24.4 13.2 %collective-permute-start = (bf16[1,2,128,1024]{3,2,1,0:T(8,128)(2,1)S(1)}, bf16[1,2,128,1024]{3,2,1,0:T(8,128)(2,1)S(1)}, u32[]{:S(2)}, u32[]{:S(2)}) collective-permute-start(bf16[1,2,128,1024]{3,2,1,0:T(8,128)(2,1)S(1)} %get-tuple-element.18), channel_id=1, source_target_pairs={{0,4},{4,0},{8,12},{12,8},{1,5},{5,1},{9,13},{13,9},{2,6},{6,2},{1... | collective-permute-start | bytes 1572872 | tf_op jit(solution)/shard_map/ppermute | solution.py:13
  66.5 24.6 %collective-permute-start.1 = (bf16[1,2,64,2048]{3,2,1,0:T(8,128)(2,1)}, bf16[1,2,64,2048]{3,2,1,0:T(8,128)(2,1)S(1)}, u32[]{:S(2)}, u32[]{:S(2)}) collective-permute-start(bf16[1,2,64,2048]{3,2,1,0:T(8,128)(2,1)} %copy.38), channel_id=1, source_target_pairs={{0,8},{4,12},{8,0},{12,4},{1,9},{5,13},{9,1},{13,5},{2,10},{6,14},... | collective-permute-start | bytes 1572872 | tf_op jit(solution)/shard_map/ppermute | solution.py:13
